TPU v7x, 128 devices: a whole 4x4x4 slice. The times are simulated.
128 devices in a mesh: expert: 8 (over z, core), ffn: 16 (over x, y).
Axes of the slice: x: 4, y: 4, z: 4, core: 2. Of those that a mesh axis runs over, the one named last changes fastest.
Arguments:
- queries: bfloat16 [512, 4096], P(('expert', 'ffn')), may hold values from -8 to 8
- new_keys: bfloat16 [512, 1024], P(('expert', 'ffn')), may hold values from -4 to 4
- new_values: bfloat16 [512, 1024], P(('expert', 'ffn')), may hold values from -5 to 5
- key_cache: bfloat16 [512, 512, 1024], P(('expert', 'ffn')), may hold values from -4 to 4
- value_cache: bfloat16 [512, 512, 1024], P(('expert', 'ffn')), may hold values from -5 to 5
- lengths: int32 [512], P(('expert', 'ffn')), may hold values from 1 to 512, 65536 in all
- residual: bfloat16 [512, 4096], P('expert', 'ffn'), may hold values from -16 to 16
- out_weight: bfloat16 [4096, 4096], P(None, 'ffn'), may hold values from -0.1875 to 0.1875
- norm_gain: float32 [4096], P('ffn'), may hold values from 0.25 to 1.75
- router: float32 [4096, 8], P('ffn'), may hold values from -0.09375 to 0.09375
- gate_weight: bfloat16 [8, 4096, 8192], P('expert', None, 'ffn'), may hold values from -0.09375 to 0.09375
- up_weight: bfloat16 [8, 4096, 8192], P('expert', None, 'ffn'), may hold values from -0.09375 to 0.09375
- down_weight: bfloat16 [8, 8192, 4096], P('expert', 'ffn'), may hold values from -0.09375 to 0.09375
- routes: int32 [512, 2], P('expert'), may hold values from 0 to 7, all different within a row; in each aligned block of 64 rows (0 to 63, 64 to 127, ...) at most 32 rows name the same one
Outputs:
- layer_out: bfloat16 [512, 4096], P('expert', 'ffn')
Inputs may be any that keep to these rules, and one draw needn't show every extreme that they name: The lengths of all 512 requests sum to 65536, and some request has exactly 512. `routes`: A request names two different experts. In each aligned block of 64 requests (the requests of one index of expert) no expert is named by more than 32 requests, a bound that some block reaches.
All inputs are finite; a program needn't handle non-finite values. No bound on the sum of `lengths` on one device may be relied on, other than what follows from the above.
Results may differ from a plain program's by a relative error of at most 0.0065.
Values may be sent and summed in bfloat16 or wider, within the bound.
No kernel may reach another device: no remote copies, remote signals or barrier semaphores. Data moves between devices by JAX's collectives and lax.ppermute only.
A program may use at most 128 MiB of HBM per device.

v0:
```python
import math
import jax
import jax.numpy as jnp
from jax import lax
from jax.sharding import PartitionSpec as P

D = 4096
QH = 32
KVH = 8
HD = 128
CACHE = 512
EPSILON = 1e-05
FLOOR = -1e30


def attend_local(queries, new_keys, new_values, key_cache, value_cache, lengths):
    request_count = queries.shape[0]
    group_size = QH // KVH
    score_scale = 1.0 / math.sqrt(HD)
    block_size = math.gcd(CACHE, 256)
    query_heads = queries.reshape(request_count, KVH, group_size, HD)
    key_view = key_cache.reshape(request_count, CACHE, KVH, HD)
    value_view = value_cache.reshape(request_count, CACHE, KVH, HD)
    score_new = (
        jnp.einsum(
            "rkgd,rkd->rkg",
            query_heads,
            new_keys.reshape(request_count, KVH, HD),
            preferred_element_type=jnp.float32,
        )
        * score_scale
    )
    value_start = jnp.broadcast_to(
        new_values.reshape(request_count, KVH, 1, HD).astype(jnp.float32),
        (request_count, KVH, group_size, HD),
    )
    initial = (score_new, jnp.ones_like(score_new), value_start)

    def block_step(block_index, carried):
        running_max, running_den, running_tot = carried
        offset = block_index * block_size
        keys_part = lax.dynamic_slice_in_dim(key_view, offset, block_size, 1)
        values_part = lax.dynamic_slice_in_dim(value_view, offset, block_size, 1)
        scores = (
            jnp.einsum(
                "rkgd,rpkd->rkgp", query_heads, keys_part, preferred_element_type=jnp.float32
            )
            * score_scale
        )
        positions = offset + jnp.arange(block_size, dtype=jnp.int32)
        live_mask = (positions[None, :] < lengths[:, None])[:, None, None, :]
        masked = jnp.where(live_mask, scores, FLOOR)
        new_max = jnp.maximum(running_max, jnp.max(masked, axis=-1))
        weights = jnp.where(live_mask, jnp.exp(masked - new_max[..., None]), 0.0)
        shrink = jnp.exp(running_max - new_max)
        new_den = running_den * shrink + jnp.sum(weights, axis=-1)
        new_tot = running_tot * shrink[..., None] + jnp.einsum(
            "rkgp,rpkd->rkgd",
            weights.astype(jnp.bfloat16),
            values_part,
            preferred_element_type=jnp.float32,
        )
        return (new_max, new_den, new_tot)

    block_total = (jnp.max(lengths) + block_size - 1) // block_size
    final_max, final_den, final_tot = lax.fori_loop(0, block_total, block_step, initial)
    return (final_tot / final_den[..., None]).astype(jnp.bfloat16).reshape(request_count, QH * HD)


def local(
    queries,
    new_keys,
    new_values,
    key_cache,
    value_cache,
    lengths,
    residual,
    out_weight,
    norm_gain,
    router,
    gate_weight,
    up_weight,
    down_weight,
    routes,
):
    attended = attend_local(queries, new_keys, new_values, key_cache, value_cache, lengths)
    hidden = residual.astype(jnp.float32) + jnp.dot(
        lax.all_gather(attended, "ffn", axis=0, tiled=True),
        out_weight,
        preferred_element_type=jnp.float32,
    )
    scaled = hidden * norm_gain
    square_part = jnp.sum(hidden * hidden, axis=-1)
    square_sum = lax.psum(square_part, "ffn")
    inverse = lax.rsqrt(square_sum / D + EPSILON)[:, None]
    logits = lax.psum(jnp.dot(scaled * inverse, router, precision=lax.Precision.HIGHEST), "ffn")
    normed = (scaled * inverse).astype(jnp.bfloat16)
    expert_count = lax.axis_size("expert")
    row_count = routes.shape[0]
    capacity = row_count // 2
    expert_ids = jnp.arange(expert_count, dtype=jnp.int32)
    chosen = routes[:, :, None] == expert_ids[None, None, :]
    picked = jnp.sum(jnp.where(chosen, logits[:, None, :], 0.0), axis=-1)
    first_weight = jax.nn.sigmoid(picked[:, 0] - picked[:, 1])
    route_weights = jnp.stack([first_weight, 1.0 - first_weight], axis=1)
    flat_hits = chosen.astype(jnp.int32).reshape(row_count * 2, expert_count)
    earlier = jnp.cumsum(flat_hits, axis=0) - flat_hits
    slots = jnp.sum(earlier * flat_hits, axis=-1).reshape(row_count, 2)
    targets = routes * capacity + slots
    slot_ids = jnp.arange(expert_count * capacity, dtype=jnp.int32)
    slot_hits = slot_ids[:, None, None] == targets[None, :, :]
    dispatch = jnp.sum(slot_hits.astype(jnp.float32), axis=-1).astype(jnp.bfloat16)
    combine = jnp.sum(jnp.where(slot_hits, route_weights[None, :, :], 0.0), axis=-1).T
    gate_local = gate_weight[0]
    up_local = up_weight[0]
    down_local = down_weight[0]
    share_rows = (
        jnp.dot(dispatch, normed, preferred_element_type=jnp.float32)
        .astype(jnp.bfloat16)
        .reshape(expert_count, capacity, normed.shape[1])
    )
    part_rows = lax.all_gather(
        lax.all_to_all(share_rows, "expert", split_axis=0, concat_axis=0, tiled=True),
        "ffn",
        axis=2,
        tiled=True,
    )
    gate_next = jnp.einsum("eck,kf->ecf", part_rows, gate_local, preferred_element_type=jnp.float32)
    up_next = jnp.einsum("eck,kf->ecf", part_rows, up_local, preferred_element_type=jnp.float32)
    inner = (jax.nn.silu(gate_next) * up_next).astype(jnp.bfloat16)
    partial_out = jnp.einsum("ecf,fd->ecd", inner, down_local, preferred_element_type=jnp.float32)
    summed = lax.psum_scatter(
        partial_out.astype(jnp.bfloat16), "ffn", scatter_dimension=2, tiled=True
    )
    returned = lax.all_to_all(summed, "expert", split_axis=0, concat_axis=0, tiled=True)
    mixed = jnp.dot(
        combine,
        returned.reshape(expert_count * capacity, -1).astype(jnp.float32),
        precision=lax.Precision.HIGHEST,
    )
    return (hidden + mixed).astype(jnp.bfloat16)


def solution(mesh):
    placed = (
        P(("expert", "ffn"), None),
        P(("expert", "ffn"), None),
        P(("expert", "ffn"), None),
        P(("expert", "ffn"), None, None),
        P(("expert", "ffn"), None, None),
        P(("expert", "ffn")),
        P("expert", "ffn"),
        P(None, "ffn"),
        P("ffn"),
        P("ffn", None),
        P("expert", None, "ffn"),
        P("expert", None, "ffn"),
        P("expert", "ffn", None),
        P("expert", None),
    )
    return jax.shard_map(
        local, mesh=mesh, in_specs=placed, out_specs=P("expert", "ffn"), check_vma=False
    )
```

profile of v0, /device:TPU:1, one launch (start us, length us, event | category | flops | bytes accessed | tf_op | source)
XLA Modules:
  0.0 292.3 jit_solution(4091025188030923789)
XLA Ops:
  6.5 1.4 reduce_max.18
  8.6 0.8 reshape.73
  9.5 0.7 reshape.91
  10.2 0.1 fusion.56
  10.3 6.2 %copy.47 = bf16[4,512,1024]{1,2,0:T(8,128)(2,1)} copy(bf16[4,512,1024]{2,1,0:T(8,128)(2,1)} %param.19) | data formatting | bytes 8388608 | tf_op args[3]
  16.5 6.2 %copy.48 = bf16[4,512,1024]{1,2,0:T(8,128)(2,1)} copy(bf16[4,512,1024]{2,1,0:T(8,128)(2,1)} %param.20) | data formatting | bytes 8388608 | tf_op args[4]
  22.8 0.0 copy-done.2
  22.8 0.0 copy-start.1
  22.9 9.4 %while.14 = (s32[]{:T(128)}, f32[4,8,4]{2,1,0:T(8,128)S(1)}, f32[4,8,4]{2,1,0:T(8,128)S(1)}, f32[4,8,4,128]{3,2,1,0:T(4,128)S(1)}, s32[]{:T(128)}, /*index=5*/s3...) while((s32[]{:T(128)}, f32[4,8,4]{2,1,0:T(8,128)S(1)}, ...), condition=%wide.region_4.5_spmd, body=%wide.region_1.4_spmd.sunk | while | flops 17106436 | bytes 4765895 | solution.py:66
  22.9 0.1 broadcast_compare_fusion.2
  23.0 2.1 fusion.77
  25.0 0.2 fusion.78
  25.3 2.3 fusion.79
  27.6 0.1 broadcast_compare_fusion.2
  27.7 2.1 fusion.77
  29.7 0.2 fusion.78
  30.0 2.3 fusion.79
  32.3 0.0 copy-start.5
  32.3 0.0 copy-start.6
  32.3 0.0 copy-start.3
  32.3 0.1 divide_convert_fusion
  32.5 19.6 %all-gather = bf16[16,4,4096]{2,1,0:T(4,128)(2,1)S(1)} all-gather(bf16[1,4,4096]{2,1,0:T(4,128)(2,1)S(1)} %reshape.82), channel_id=1, replica_groups=mesh['expert'=8,'ffn'=16] {'ffn'}, dimensions={0}, use_global_device_ids=true | all-gather | bytes 557056 | tf_op jit(solution)/shard_map/all_gather | solution.py:88
  52.0 0.1 reshape.83
  52.2 0.6 multiply_reduce_fusion
  52.8 30.9 %psum.14 = f32[64]{0:T(128)S(1)} all-reduce(f32[64]{0:T(128)S(1)} %get-tuple-element.118), channel_id=1, replica_groups=mesh['expert'=8,'ffn'=16] {'ffn'}, use_global_device_ids=true, to_apply=%region_8.9 | all-reduce | flops 64 | bytes 512 | tf_op jit(solution)/shard_map/psum | solution.py:94
  83.7 0.0 copy-done.6
  83.7 0.2 fusion.47
  83.9 28.5 %psum.15 = f32[64,8]{0,1:T(8,128)S(1)} all-reduce(f32[64,8]{0,1:T(8,128)S(1)} %fusion.47), channel_id=1, replica_groups=mesh['expert'=8,'ffn'=16] {'ffn'}, use_global_device_ids=true, to_apply=%region_9.10 | all-reduce | flops 512 | bytes 4096 | tf_op jit(solution)/shard_map/psum | solution.py:96
  112.4 0.0 copy-done.3
  112.4 0.1 copy.51
  112.5 0.1 eq.36
  112.7 0.1 fusion.45
  112.8 0.2 reduce_window_sum.11
  112.9 0.2 select_reduce_fusion.1
  113.1 0.1 reshape.78
  113.3 0.1 copy.52
  113.4 0.1 convert_reduce_fusion
  113.5 0.2 convolution_convert_fusion.1
  113.7 30.9 %all_to_all.10 = bf16[8,32,256]{2,1,0:T(8,128)(2,1)} all-to-all(bf16[8,32,256]{2,1,0:T(8,128)(2,1)S(1)} %bitcast.46), channel_id=1, replica_groups=mesh['expert'=8,'ffn'=16] {'expert'}, dimensions={0} | all-to-all | bytes 262144 | tf_op jit(solution)/shard_map/all_to_all | solution.py:123
  144.6 0.0 all-gather.3.cloned.1.call-update
  144.6 0.0 reduce-scatter.2.cloned.1.call-start
  144.7 41.4 %all-gather.3.cloned.1.call-done = bf16[8,32,4096]{2,1,0:T(8,128)(2,1)} async-done(((bf16[8,32,256]{2,1,0:T(8,128)(2,1)}), bf16[8,32,4096]{2,1,0:T(8,128)(2,1)}) %all-gather.3.cloned.1.call-update) | async-done | bytes 2097168 | tf_op jit(solution)/shard_map/all_gather | solution.py:122
  186.1 4.1 %fusion.28 = f32[8,32,512]{2,1,0:T(8,128)S(1)} fusion(bf16[8,32,4096]{2,1,0:T(8,128)(2,1)} %all-gather.3.cloned.1.call-done, bf16[1,4096,512]{2,1,0:T(8,128)(2,1)} %param.26), kind=kOutput, calls=%fused_computation.25 | convolution fusion | flops 1073741824 | bytes 6815744 | tf_op jit(solution)/shard_map/eck,kf->ecf/dot_general | solution.py:128
  190.2 7.8 %convolution_convert_fusion = bf16[8,32,4096]{2,1,0:T(8,128)(2,1)} fusion(bf16[1,512,4096]{2,1,0:T(8,128)(2,1)} %param.28, bf16[8,32,4096]{2,1,0:T(8,128)(2,1)} %all-gather.3.cloned.1.call-done, bf16[1,4096,512]{2,1,0:T(8,128)(2,1)} %param.27, f32[8,32,512]{2,1,0:T(8,128)S(1)} %fusion.28), kind=kOutput, calls=%fused_computation.21 | convolution fusion | flops 2149318656 | bytes 13107200 | tf_op jit(solution)/shard_map/ecf,fd->ecd/dot_general | solution.py:131
  198.0 0.0 reduce-scatter.2.cloned.1.call-update
  198.0 74.6 %reduce-scatter.2.cloned.1.call-done = bf16[8,32,256]{2,1,0:T(8,128)(2,1)} async-done(((bf16[8,32,4096]{2,1,0:T(8,128)(2,1)}), bf16[8,32,256]{2,1,0:T(8,128)(2,1)}) %reduce-scatter.2.cloned.1.call-update) | async-done | bytes 131088 | tf_op jit(solution)/shard_map/reduce_scatter | solution.py:132
  272.7 12.0 %all_to_all.11 = bf16[8,32,256]{2,1,0:T(8,128)(2,1)S(1)} all-to-all(bf16[8,32,256]{2,1,0:T(8,128)(2,1)} %reduce-scatter.2.cloned.1.call-done), channel_id=1, replica_groups=mesh['expert'=8,'ffn'=16] {'expert'}, dimensions={0} | all-to-all | bytes 262144 | tf_op jit(solution)/shard_map/all_to_all | solution.py:135
  284.6 0.8 fusion.36
  (27 shorter events, 0.2 us)
Async XLA Ops:
  6.5 45.6 %copy-start = (bf16[4096,256]{1,0:T(8,128)(2,1)S(1)}, bf16[4096,256]{1,0:T(8,128)(2,1)}, u32[]{:S(2)}) copy-start(bf16[4096,256]{1,0:T(8,128)(2,1)} %param.23) | copy-start | bytes 6291460
  6.5 179.6 %all-gather.3.cloned.1.call-start = ((), (), s32[]{:S(2)}) async-start(), calls=%async_computation.3 | async-start | bytes 2228224 | tf_op jit(solution)/shard_map/all_gather | solution.py:122
  16.5 6.2 %copy-start.4 = (bf16[4,1024]{1,0:T(4,128)(2,1)S(1)}, bf16[4,1024]{1,0:T(4,128)(2,1)}, u32[]{:S(2)}) copy-start(bf16[4,1024]{1,0:T(4,128)(2,1)} %param.18) | copy-start | bytes 24580
  16.5 6.3 %copy-start.2 = (s32[4]{0:T(128)S(1)}, s32[4]{0:T(128)}, u32[]{:S(2)}) copy-start(s32[4]{0:T(128)} %param.21) | copy-start | bytes 52
  22.8 29.3 %copy-start.1 = (bf16[64,256]{1,0:T(8,128)(2,1)S(1)}, bf16[64,256]{1,0:T(8,128)(2,1)}, u32[]{:S(2)}) copy-start(bf16[64,256]{1,0:T(8,128)(2,1)} %param.22) | copy-start | bytes 98308
  32.3 51.4 %copy-start.5 = (f32[256,8]{0,1:T(8,128)S(1)}, f32[256,8]{0,1:T(8,128)}, u32[]{:S(2)}) copy-start(f32[256,8]{0,1:T(8,128)} %param.25) | copy-start | bytes 24580
  32.3 51.3 %copy-start.6 = (f32[256]{0:T(256)S(1)}, f32[256]{0:T(256)}, u32[]{:S(2)}) copy-start(f32[256]{0:T(256)} %param.24) | copy-start | bytes 3076
  32.3 80.1 %copy-start.3 = (s32[64,2]{0,1:T(2,128)S(1)}, s32[64,2]{0,1:T(2,128)}, u32[]{:S(2)}) copy-start(s32[64,2]{0,1:T(2,128)} %param.29) | copy-start | bytes 1540
  144.6 128.0 %reduce-scatter.2.cloned.1.call-start = ((), (), s32[]{:S(2)}) async-start(), calls=%async_computation.4 | async-start | bytes 2228224 | tf_op jit(solution)/shard_map/reduce_scatter | solution.py:132
Sparse Core Ops, SparseCore 0:
  144.8 41.3 all-gather.2
  198.1 74.4 reduce-scatter.1
where the time goes:
time: 293 us; the launch traced here: 292 us
  blocking collectives  122 us (42%)
  waiting for transfers between devices  116 us (40%)
  matrix products  22.6 us (8%)
  local copies, waits for them, and re-layouts  14.6 us (5%)
  between operations  14.3 us (5%)
    reduce_scatter x1, waiting for transfers between devices, local(): lax.psum_scatter(partial_out.astype(jnp.bfloat16), 'ffn', scatter_dimensi...  74.6 us
    all_gather x1, waiting for transfers between devices, local(): lax.all_gather(lax.all_to_all(share_rows, 'expert', split_axis=0, concat_...  41.4 us
    all_to_all x1, blocking collectives, local(): lax.all_to_all(share_rows, 'expert', split_axis=0, concat_axis=0, tiled=T...  30.9 us
    psum x1, blocking collectives, local(): square_sum = lax.psum(square_part, 'ffn')  30.9 us
    psum x1, blocking collectives, local(): lax.psum(jnp.dot(scaled * inverse, router, precision=lax.Precision.HIGHES...  28.5 us
    all_gather x1, blocking collectives, local(): lax.all_gather(attended, 'ffn', axis=0, tiled=True)  19.6 us
    unnamed x20, local copies, waits for them, and re-layouts  12.7 us
    all_to_all x1, blocking collectives, local(): lax.all_to_all(summed, 'expert', split_axis=0, concat_axis=0, tiled=True)  12 us
  transfers between devices with their start and end apart: 2, of which 2 were waited for; matrix products, arithmetic and copies ran while one was open for 0% of the time, Pallas kernels for 0%

commit v1 on v0

--- a/solution.py
+++ b/solution.py
@@ -11,6 +11,14 @@
 CACHE = 512
 EPSILON = 1e-05
 FLOOR = -1e30
+
+
+def added_up(x, name):
+    size, result = (lax.axis_size(name), x)
+    for stride in [1 << k for k in range(size.bit_length() - 1)]:
+        pairs = [(i, i ^ stride) for i in range(size)]
+        result = result + lax.ppermute(result, name, pairs)
+    return result
 
 
 def attend_local(queries, new_keys, new_values, key_cache, value_cache, lengths):
@@ -91,7 +99,7 @@
     )
     scaled = hidden * norm_gain
     square_part = jnp.sum(hidden * hidden, axis=-1)
-    square_sum = lax.psum(square_part, "ffn")
+    square_sum = added_up(square_part, "ffn")
     inverse = lax.rsqrt(square_sum / D + EPSILON)[:, None]
     logits = lax.psum(jnp.dot(scaled * inverse, router, precision=lax.Precision.HIGHEST), "ffn")
     normed = (scaled * inverse).astype(jnp.bfloat16)

time: 293 us -> 273 us (0.932)
  blocking collectives: 122 us -> 90.7 us
  waiting for transfers between devices: 116 us -> 122 us
  starting transfers between devices: 0.04 us -> 4.69 us
    psum x1 -> x0, blocking collectives: 30.9 us -> none  [local(): square_sum = lax.psum(square_part, 'ffn')]
    ppermute x0 -> x4, waiting for transfers between devices: none -> 7.52 us  [added_up(): result = result + lax.ppermute(result, name, pairs)]
    ppermute x0 -> x4, starting transfers between devices: none -> 4.64 us  [added_up(): result = result + lax.ppermute(result, name, pairs)]
  transfers between devices with their start and end apart: 2 -> 6, of which waited for: 2 -> 6; matrix products, arithmetic and copies ran while one was open for 0% -> 0% of each run, Pallas kernels for 0% -> 0%
where the time goes in v1:
time: 273 us; the launch traced here: 272 us
  waiting for transfers between devices  122 us (45%)
  blocking collectives  90.7 us (33%)
  matrix products  22.5 us (8%)
  local copies, waits for them, and re-layouts  14.6 us (5%)
  between operations  14.3 us (5%)
  starting transfers between devices  4.69 us (2%)
  other arithmetic  2.77 us (1%)
    reduce_scatter x1, waiting for transfers between devices, local(): lax.psum_scatter(partial_out.astype(jnp.bfloat16), 'ffn', scatter_dimensi...  74.6 us
    all_gather x1, waiting for transfers between devices, local(): lax.all_gather(lax.all_to_all(share_rows, 'expert', split_axis=0, concat_...  40 us
    psum x1, blocking collectives, local(): lax.psum(jnp.dot(scaled * inverse, router, precision=lax.Precision.HIGHES...  30.9 us
    all_to_all x1, blocking collectives, local(): lax.all_to_all(share_rows, 'expert', split_axis=0, concat_axis=0, tiled=T...  28.2 us
    all_gather x1, blocking collectives, local(): lax.all_gather(attended, 'ffn', axis=0, tiled=True)  19.6 us
    unnamed x20, local copies, waits for them, and re-layouts  12.7 us
    all_to_all x1, blocking collectives, local(): lax.all_to_all(summed, 'expert', split_axis=0, concat_axis=0, tiled=True)  12 us
    dot_general x1, matrix products, local(): jnp.einsum('ecf,fd->ecd', inner, down_local, preferred_element_type=jnp.f...  7.79 us
  transfers between devices with their start and end apart: 6, of which 6 were waited for; matrix products, arithmetic and copies ran while one was open for 0% of the time, Pallas kernels for 0%

profile of v1, /device:TPU:1, one launch (start us, length us, event | category | flops | bytes accessed | tf_op | source)
XLA Modules:
  0.0 271.8 jit_solution(5912835144680152855)
XLA Ops:
  6.5 1.4 reduce_max.18
  8.6 0.8 reshape.73
  9.5 0.7 reshape.91
  10.2 0.1 fusion.56
  10.3 6.2 %copy.47 = bf16[4,512,1024]{1,2,0:T(8,128)(2,1)} copy(bf16[4,512,1024]{2,1,0:T(8,128)(2,1)} %param.19) | data formatting | bytes 8388608 | tf_op args[3]
  16.5 6.2 %copy.48 = bf16[4,512,1024]{1,2,0:T(8,128)(2,1)} copy(bf16[4,512,1024]{2,1,0:T(8,128)(2,1)} %param.20) | data formatting | bytes 8388608 | tf_op args[4]
  22.9 9.4 %while.14 = (s32[]{:T(128)}, f32[4,8,4]{2,1,0:T(8,128)S(1)}, f32[4,8,4]{2,1,0:T(8,128)S(1)}, f32[4,8,4,128]{3,2,1,0:T(4,128)S(1)}, s32[]{:T(128)}, /*index=5*/s3...) while((s32[]{:T(128)}, f32[4,8,4]{2,1,0:T(8,128)S(1)}, ...), condition=%wide.region_4.5_spmd, body=%wide.region_1.4_spmd.sunk | while | flops 17106436 | bytes 4765895 | solution.py:74
  22.9 0.1 broadcast_compare_fusion.2
  23.0 2.1 fusion.77
  25.0 0.2 fusion.78
  25.3 2.3 fusion.79
  27.6 0.1 broadcast_compare_fusion.2
  27.7 2.1 fusion.77
  29.7 0.2 fusion.78
  30.0 2.3 fusion.79
  32.3 0.1 divide_convert_fusion
  32.5 19.6 %all-gather = bf16[16,4,4096]{2,1,0:T(4,128)(2,1)S(1)} all-gather(bf16[1,4,4096]{2,1,0:T(4,128)(2,1)S(1)} %reshape.82), channel_id=1, replica_groups=mesh['expert'=8,'ffn'=16] {'ffn'}, dimensions={0}, use_global_device_ids=true | all-gather | bytes 557056 | tf_op jit(solution)/shard_map/all_gather | solution.py:96
  52.0 0.1 reshape.83
  52.2 0.6 multiply_reduce_fusion
  52.8 1.0 collective-permute-start
  53.8 0.1 copy.51
  53.9 0.1 eq.36
  54.0 1.5 collective-permute-done
  55.5 1.4 collective-permute-start.1
  56.9 0.1 fusion.45
  57.0 0.2 reduce_window_sum.11
  57.2 2.3 collective-permute-done.1
  59.5 0.6 collective-permute-start.2
  60.1 0.2 select_reduce_fusion.1
  60.2 0.1 reshape.78
  60.4 0.1 copy.52
  60.4 1.5 collective-permute-done.2
  61.9 1.7 collective-permute-start.3
  63.6 2.3 collective-permute-done.3
  65.8 0.2 fusion.47
  66.1 30.9 %psum.7 = f32[64,8]{0,1:T(8,128)S(1)} all-reduce(f32[64,8]{0,1:T(8,128)S(1)} %fusion.47), channel_id=1, replica_groups=mesh['expert'=8,'ffn'=16] {'ffn'}, use_global_device_ids=true, to_apply=%region_8.9 | all-reduce | flops 512 | bytes 4096 | tf_op jit(solution)/shard_map/psum | solution.py:104
  97.0 0.1 convert_reduce_fusion
  97.1 0.2 convolution_convert_fusion.1
  97.4 28.2 %all_to_all.10 = bf16[8,32,256]{2,1,0:T(8,128)(2,1)} all-to-all(bf16[8,32,256]{2,1,0:T(8,128)(2,1)S(1)} %bitcast.46), channel_id=1, replica_groups=mesh['expert'=8,'ffn'=16] {'expert'}, dimensions={0} | all-to-all | bytes 262144 | tf_op jit(solution)/shard_map/all_to_all | solution.py:131
  125.6 0.0 all-gather.3.cloned.1.call-update
  125.6 0.0 reduce-scatter.2.cloned.1.call-start
  125.7 40.0 %all-gather.3.cloned.1.call-done = bf16[8,32,4096]{2,1,0:T(8,128)(2,1)} async-done(((bf16[8,32,256]{2,1,0:T(8,128)(2,1)}), bf16[8,32,4096]{2,1,0:T(8,128)(2,1)}) %all-gather.3.cloned.1.call-update) | async-done | bytes 2097168 | tf_op jit(solution)/shard_map/all_gather | solution.py:130
  165.7 4.1 %fusion.28 = f32[8,32,512]{2,1,0:T(8,128)S(1)} fusion(bf16[8,32,4096]{2,1,0:T(8,128)(2,1)} %all-gather.3.cloned.1.call-done, bf16[1,4096,512]{2,1,0:T(8,128)(2,1)} %param.26), kind=kOutput, calls=%fused_computation.25 | convolution fusion | flops 1073741824 | bytes 6815744 | tf_op jit(solution)/shard_map/eck,kf->ecf/dot_general | solution.py:136
  169.7 7.8 %convolution_convert_fusion = bf16[8,32,4096]{2,1,0:T(8,128)(2,1)} fusion(bf16[1,512,4096]{2,1,0:T(8,128)(2,1)} %param.28, bf16[8,32,4096]{2,1,0:T(8,128)(2,1)} %all-gather.3.cloned.1.call-done, bf16[1,4096,512]{2,1,0:T(8,128)(2,1)} %param.27, f32[8,32,512]{2,1,0:T(8,128)S(1)} %fusion.28), kind=kOutput, calls=%fused_computation.21 | convolution fusion | flops 2149318656 | bytes 13107200 | tf_op jit(solution)/shard_map/ecf,fd->ecd/dot_general | solution.py:139
  177.5 0.0 reduce-scatter.2.cloned.1.call-update
  177.6 74.6 %reduce-scatter.2.cloned.1.call-done = bf16[8,32,256]{2,1,0:T(8,128)(2,1)} async-done(((bf16[8,32,4096]{2,1,0:T(8,128)(2,1)}), bf16[8,32,256]{2,1,0:T(8,128)(2,1)}) %reduce-scatter.2.cloned.1.call-update) | async-done | bytes 131088 | tf_op jit(solution)/shard_map/reduce_scatter | solution.py:140
  252.2 12.0 %all_to_all.11 = bf16[8,32,256]{2,1,0:T(8,128)(2,1)S(1)} all-to-all(bf16[8,32,256]{2,1,0:T(8,128)(2,1)} %reduce-scatter.2.cloned.1.call-done), channel_id=1, replica_groups=mesh['expert'=8,'ffn'=16] {'expert'}, dimensions={0} | all-to-all | bytes 262144 | tf_op jit(solution)/shard_map/all_to_all | solution.py:143
  264.2 0.8 fusion.36
  (37 shorter events, 0.2 us)
Async XLA Ops:
  6.5 45.6 %copy-start = (bf16[4096,256]{1,0:T(8,128)(2,1)S(1)}, bf16[4096,256]{1,0:T(8,128)(2,1)}, u32[]{:S(2)}) copy-start(bf16[4096,256]{1,0:T(8,128)(2,1)} %param.23) | copy-start | bytes 6291460
  6.5 159.1 %all-gather.3.cloned.1.call-start = ((), (), s32[]{:S(2)}) async-start(), calls=%async_computation.3 | async-start | bytes 2228224 | tf_op jit(solution)/shard_map/all_gather | solution.py:130
  16.5 6.2 %copy-start.4 = (bf16[4,1024]{1,0:T(4,128)(2,1)S(1)}, bf16[4,1024]{1,0:T(4,128)(2,1)}, u32[]{:S(2)}) copy-start(bf16[4,1024]{1,0:T(4,128)(2,1)} %param.18) | copy-start | bytes 24580
  16.5 6.3 %copy-start.2 = (s32[4]{0:T(128)S(1)}, s32[4]{0:T(128)}, u32[]{:S(2)}) copy-start(s32[4]{0:T(128)} %param.21) | copy-start | bytes 52
  22.8 29.3 %copy-start.1 = (bf16[64,256]{1,0:T(8,128)(2,1)S(1)}, bf16[64,256]{1,0:T(8,128)(2,1)}, u32[]{:S(2)}) copy-start(bf16[64,256]{1,0:T(8,128)(2,1)} %param.22) | copy-start | bytes 98308
  32.3 21.5 %copy-start.3 = (s32[64,2]{0,1:T(2,128)S(1)}, s32[64,2]{0,1:T(2,128)}, u32[]{:S(2)}) copy-start(s32[64,2]{0,1:T(2,128)} %param.29) | copy-start | bytes 1540
  32.3 33.5 %copy-start.5 = (f32[256,8]{0,1:T(8,128)S(1)}, f32[256,8]{0,1:T(8,128)}, u32[]{:S(2)}) copy-start(f32[256,8]{0,1:T(8,128)} %param.25) | copy-start | bytes 24580
  32.3 33.5 %copy-start.6 = (f32[256]{0:T(256)S(1)}, f32[256]{0:T(256)}, u32[]{:S(2)}) copy-start(f32[256]{0:T(256)} %param.24) | copy-start | bytes 3076
  52.8 2.8 %collective-permute-start = (f32[64]{0:T(128)S(1)}, f32[64]{0:T(128)S(1)}, u32[]{:S(2)}, u32[]{:S(2)}) collective-permute-start(f32[64]{0:T(128)S(1)} %get-tuple-element.118), channel_id=1, source_target_pairs={{0,1},{1,0},{2,3},{3,2},{4,5},{5,4},{6,7},{7,6},{8,9},{9,8},{10,11... | collective-permute-start | bytes 776 | tf_op jit(solution)/shard_map/ppermute | solution.py:20
  55.5 3.9 %collective-permute-start.1 = (f32[64]{0:T(128)S(1)}, f32[64]{0:T(128)S(1)}, u32[]{:S(2)}, u32[]{:S(2)}) collective-permute-start(f32[64]{0:T(128)S(1)} %add.70), channel_id=1, source_target_pairs={{0,2},{1,3},{2,0},{3,1},{4,6},{5,7},{6,4},{7,5},{8,10},{9,11},{10,... | collective-permute-start | bytes 776 | tf_op jit(solution)/shard_map/ppermute | solution.py:20
  59.5 2.4 collective-permute-start.2
  61.9 3.9 %collective-permute-start.3 = (f32[64]{0:T(128)S(1)}, f32[64]{0:T(128)S(1)}, u32[]{:S(2)}, u32[]{:S(2)}) collective-permute-start(f32[64]{0:T(128)S(1)} %add.72), channel_id=1, source_target_pairs={{0,8},{1,9},{2,10},{3,11},{4,12},{5,13},{6,14},{7,15},{8,0},{9,1},... | collective-permute-start | bytes 776 | tf_op jit(solution)/shard_map/ppermute | solution.py:20
  125.6 126.6 %reduce-scatter.2.cloned.1.call-start = ((), (), s32[]{:S(2)}) async-start(), calls=%async_computation.4 | async-start | bytes 2228224 | tf_op jit(solution)/shard_map/reduce_scatter | solution.py:140
Sparse Core Ops, SparseCore 0:
  125.8 39.8 all-gather.2
  177.7 74.4 reduce-scatter.1
